TPU v7x, 512 devices: a whole 4x4x16 slice. The times are simulated.
512 devices in a mesh: row: 32 (over x_lo, z), col: 16 (over x_hi, y, core).
Axes of the slice: x: 4 (x_hi: 2, x_lo: 2; x = x_hi * 2 + x_lo), y: 4, z: 16, core: 2. Of those that a mesh axis runs over, the one named last changes fastest.
Arguments:
- anc_inv: float32 [12288, 12288], P('row', 'col'), may hold values from -0.0546875 to 0.0546875
- factors_first: float32 [3, 256, 12288], P(None, 'row', 'col'), may hold values from -6 to 6
- factors_second: float32 [2, 256, 12288], P(None, 'row', 'col'), may hold values from -6 to 6
- lists_first: int32 [3, 36], replicated, may hold values from 0 to 47, as said below
- lists_second: int32 [2, 36], replicated, may hold values from 0 to 47, as said below
- parents: int32 [2], replicated, may hold values from 0 to 2, as said below
- parent_link: float32 [2, 256, 256], replicated, may hold values from -0.375 to 0.375
Outputs:
- first_cols: float32 [3, 256, 12288], P(None, 'col', 'row')
- second_cols: float32 [2, 256, 12288], P(None, 'col', 'row')
Inputs may be any that keep to these rules, and one draw needn't show every extreme that they name: `lists_first`: each row holds 36 different tile indices. `lists_second`: each row holds 36 different tile indices. `parents`: the 2 entries are different first-generation indices.
All inputs are finite; a program needn't handle non-finite values.
Results may differ from a plain program's by a relative error of at most 0.000084.
Values sent between devices are 32-bit elements; how exact they have to be, the bound alone decides.
No kernel may reach another device: no remote copies, remote signals or barrier semaphores. Data moves between devices by JAX's collectives and lax.ppermute only.
A program may use at most 64 MiB of HBM per device.

v0:
```python
import jax
import jax.numpy as jnp
from jax import lax
from jax.sharding import PartitionSpec as P

highest = lax.Precision.HIGHEST


def tile_flags(block_lists, anchor, extent, tile_height):
    tile_ids = (anchor + jnp.arange(extent, dtype=jnp.int32)) // tile_height
    matches = block_lists[:, :, None] == tile_ids[None, None, :]
    return jnp.any(matches, axis=1).astype(jnp.float32)


def local(anc_inv, factors_first, factors_second, lists_first, lists_second, parents, parent_link):
    local_rows, local_cols = anc_inv.shape
    n_first = factors_first.shape[0]
    n_second = factors_second.shape[0]
    members = n_first + n_second
    share_rows = factors_first.shape[1]
    panel_width = parent_link.shape[1]
    row_anchor = lax.axis_index("row") * local_rows
    col_anchor = lax.axis_index("col") * local_cols
    out_first = tile_flags(lists_first, row_anchor, local_rows, panel_width)
    out_second = tile_flags(lists_second, row_anchor, local_rows, panel_width)
    panels = jnp.concatenate(
        [
            factors_first
            * tile_flags(lists_first, col_anchor, local_cols, panel_width)[:, None, :],
            factors_second
            * tile_flags(lists_second, col_anchor, local_cols, panel_width)[:, None, :],
        ],
        axis=0,
    )
    stacked = jnp.transpose(panels, (1, 0, 2)).reshape(share_rows, members * local_cols)
    gathered = lax.all_gather(stacked, "row", axis=0, tiled=True)
    gathered = gathered.reshape(panel_width, members, local_cols)
    partial_value = jnp.einsum(
        "kmj,ij->mki", gathered, anc_inv, precision=highest, preferred_element_type=jnp.float32
    )
    first_partial = partial_value[:n_first]
    second_partial = partial_value[n_first:]
    chosen = jnp.take(first_partial, parents, axis=0)
    chosen_mask = jnp.take(out_first, parents, axis=0)
    coupling = jnp.einsum("cqk,cqi->cki", parent_link, chosen, precision=highest)
    second_partial = second_partial - chosen_mask[:, None, :] * coupling
    combined = jnp.concatenate([first_partial, second_partial], axis=0)
    reduced = lax.psum_scatter(combined, "col", scatter_dimension=1, tiled=True)
    first_cols = -out_first[:, None, :] * reduced[:n_first]
    second_cols = -out_second[:, None, :] * reduced[n_first:]
    return (first_cols, second_cols)


def solution(mesh):
    in_specs = (P("row", "col"), P(None, "row", "col"), P(None, "row", "col"), P(), P(), P(), P())
    out_specs = (P(None, "col", "row"), P(None, "col", "row"))
    return jax.shard_map(local, mesh=mesh, in_specs=in_specs, out_specs=out_specs, check_vma=False)
```

profile of v0, /device:TPU:8, one launch (start us, length us, event | category | flops | bytes accessed | tf_op | source)
XLA Modules:
  0.0 276.0 jit_solution(1879956316999210277)
XLA Ops:
  7.2 0.9 compare_reduce_fusion
  8.2 0.8 compare_reduce_fusion.1
  9.0 0.9 broadcast_multiply_fusion
  9.9 0.8 broadcast_multiply_fusion.1
  10.7 0.6 pad_maximum_fusion.1
  11.3 0.0 reduce-scatter.2.cloned.1.call-start
  11.4 0.8 compare_reduce_fusion.2
  12.2 0.7 compare_select_fusion
  12.9 0.6 gather_fusion
  13.4 0.7 compare_and_fusion
  14.1 0.1 broadcast_select_fusion
  14.2 139.4 %all-gather.2.cloned.1.call-done = f32[256,3840]{1,0:T(8,128)} async-done(((f32[8,3840]{1,0:T(8,128)}), f32[256,3840]{1,0:T(8,128)}) %all-gather.2.cloned.1.call-update) | async-done | bytes 3932176 | tf_op jit(solution)/shard_map/all_gather | solution.py:36
  153.6 5.4 %copy.19 = f32[256,3840]{0,1:T(8,128)} copy(f32[256,3840]{1,0:T(8,128)} %all-gather.2.cloned.1.call-done) | data formatting | bytes 7864320 | tf_op jit(solution)/shard_map/all_gather | solution.py:36
  159.1 14.7 %convolution_bitcast_fusion = f32[5,256,384]{2,1,0:T(8,128)S(1)} fusion(f32[256,5,768]{0,2,1:T(8,128)} %bitcast.15, f32[384,768]{1,0:T(8,128)S(1)} %copy-done), kind=kOutput, calls=%fused_computation.3 | convolution fusion | flops 4529848320 | bytes 7077888 | tf_op jit(solution)/shard_map/kmj,ij->mki/dot_general | solution.py:38
  173.8 1.3 copy-done.1
  175.1 0.1 slice.20
  175.1 0.6 gather_fusion.1
  175.8 2.5 fusion.1
  178.3 1.4 pad_maximum_fusion
  179.7 0.7 copy-done.2
  180.4 0.1 compare_reduce_fusion.3
  180.5 85.7 %reduce-scatter.2.cloned.1.call-done = f32[5,16,384]{2,1,0:T(8,128)} async-done(((f32[5,256,384]{2,1,0:T(8,128)}), f32[5,16,384]{2,1,0:T(8,128)}) %reduce-scatter.2.cloned.1.call-update) | async-done | bytes 122896 | tf_op jit(solution)/shard_map/reduce_scatter | solution.py:48
  266.2 1.5 slice_multiply_fusion
  267.7 1.4 slice_multiply_fusion.1
  (15 shorter events, 0.1 us)
Async XLA Ops:
  7.2 151.9 %copy-start = (f32[384,768]{1,0:T(8,128)S(1)}, f32[384,768]{1,0:T(8,128)}, u32[]{:S(2)}) copy-start(f32[384,768]{1,0:T(8,128)} %param.7) | copy-start | bytes 3538948
  7.2 146.4 %all-gather.2.cloned.1.call-start = ((), (), s32[]{:S(2)}) async-start(), calls=%async_computation.1 | async-start | bytes 4055040 | tf_op jit(solution)/shard_map/all_gather | solution.py:36
  11.3 254.9 %reduce-scatter.2.cloned.1.call-start = ((), (), s32[]{:S(2)}) async-start(), calls=%async_computation.2 | async-start | bytes 2088960 | tf_op jit(solution)/shard_map/reduce_scatter | solution.py:48
  173.8 1.3 copy-start.1
  179.7 0.7 copy-start.2
Sparse Core Ops, SparseCore 0:
  11.5 142.1 all-gather.1
  179.8 86.3 reduce-scatter.1
where the time goes:
time: 277 us; the launch traced here: 276 us
  waiting for transfers between devices  225 us (81%)
  matrix products  17.2 us (6%)
  between operations  14.2 us (5%)
  other arithmetic  10.7 us (4%)
  local copies, waits for them, and re-layouts  8.62 us (3%)
    all_gather x1, waiting for transfers between devices, local(): gathered = lax.all_gather(stacked, 'row', axis=0, tiled=True)  139 us
    reduce_scatter x1, waiting for transfers between devices, local(): reduced = lax.psum_scatter(combined, 'col', scatter_dimension=1, tiled=True)  85.7 us
    dot_general x1, matrix products, local(): jnp.einsum('kmj,ij->mki', gathered, anc_inv, precision=highest, preferred...  14.7 us
  transfers between devices with their start and end apart: 2, of which 2 were waited for; matrix products, arithmetic and copies ran while one was open for 1% of the time, Pallas kernels for 0%

commit v1 on v0

--- a/solution.py
+++ b/solution.py
@@ -33,7 +33,9 @@
         axis=0,
     )
     stacked = jnp.transpose(panels, (1, 0, 2)).reshape(share_rows, members * local_cols)
-    gathered = lax.all_gather(stacked, "row", axis=0, tiled=True)
+    gathered = jnp.concatenate(
+        lax.all_to_all(jnp.stack([stacked] * lax.axis_size("row")), "row", 0, 0), axis=0
+    )
     gathered = gathered.reshape(panel_width, members, local_cols)
     partial_value = jnp.einsum(
         "kmj,ij->mki", gathered, anc_inv, precision=highest, preferred_element_type=jnp.float32

time: 277 us -> 326 us (1.18)
  waiting for transfers between devices: 225 us -> 263 us
  starting transfers between devices: 0.08 us -> 16.7 us
  matrix products: 17.2 us -> 12.1 us
    all_to_all x0 -> x1, waiting for transfers between devices: none -> 173 us  [local(): lax.all_to_all(jnp.stack([stacked] * lax.axis_size('row')), 'row', 0, 0)]
    all_gather x1 -> x0, waiting for transfers between devices: 139 us -> none  [local(): gathered = lax.all_gather(stacked, 'row', axis=0, tiled=True)]
    all_to_all x0 -> x1, starting transfers between devices: none -> 16.7 us  [local(): lax.all_to_all(jnp.stack([stacked] * lax.axis_size('row')), 'row', 0, 0)]
    another operation x0 -> x2, local copies, waits for them, and re-layouts: none -> 8.23 us  [the longest x1 6.1 us: local(): gathered = gathered.reshape(panel_width, members, local_cols)]
    all_gather x1 -> x0, local copies, waits for them, and re-layouts: 5.45 us -> none  [local(): gathered = lax.all_gather(stacked, 'row', axis=0, tiled=True)]
    dot_general x1, matrix products: 14.7 us -> 9.62 us  [local(): jnp.einsum('kmj,ij->mki', gathered, anc_inv, precision=highest, preferred...]
    reduce_scatter x1, waiting for transfers between devices: 85.7 us -> 90.2 us  [local(): reduced = lax.psum_scatter(combined, 'col', scatter_dimension=1, tiled=True)]
  transfers between devices with their start and end apart: 2 -> 2, of which waited for: 2 -> 2; matrix products, arithmetic and copies ran while one was open for 1% -> 0% of each run, Pallas kernels for 0% -> 0%
where the time goes in v1:
time: 326 us
  waiting for transfers between devices  263 us (81%)
  starting transfers between devices  16.7 us (5%)
  between operations  14.2 us (4%)
  matrix products  12.1 us (4%)
  local copies, waits for them, and re-layouts  11.4 us (3%)
  other arithmetic  8.11 us (2%)
    all_to_all x1, waiting for transfers between devices, local(): lax.all_to_all(jnp.stack([stacked] * lax.axis_size('row')), 'row', 0, 0)  173 us
    reduce_scatter x1, waiting for transfers between devices, local(): reduced = lax.psum_scatter(combined, 'col', scatter_dimension=1, tiled=True)  90.2 us
    all_to_all x1, starting transfers between devices, local(): lax.all_to_all(jnp.stack([stacked] * lax.axis_size('row')), 'row', 0, 0)  16.7 us
    dot_general x1, matrix products, local(): jnp.einsum('kmj,ij->mki', gathered, anc_inv, precision=highest, preferred...  9.62 us
  transfers between devices with their start and end apart: 2, of which 2 were waited for; matrix products, arithmetic and copies ran while one was open for 0% of the time, Pallas kernels for 0%

profile of v1, /device:TPU:8, one launch (start us, length us, event | category | flops | bytes accessed | tf_op | source)
XLA Modules:
  0.0 325.5 jit_solution(8689190173792072859)
XLA Ops:
  7.2 0.9 compare_reduce_fusion
  8.1 0.8 compare_reduce_fusion.1
  8.9 0.9 broadcast_multiply_fusion
  9.8 0.8 broadcast_multiply_fusion.1
  10.6 2.1 stack.3
  12.8 16.7 %all-to-all-start = ((f32[32,8,3840]{2,1,0:T(8,128)}), f32[32,8,3840]{2,1,0:T(8,128)}, u32[]{:S(2)}, u32[]{:S(2)}) async-start(f32[32,8,3840]{2,1,0:T(8,128)} %stack.3), calls=%async_computation | async-start | bytes 7864320 | tf_op jit(solution)/shard_map/all_to_all | solution.py:37
  29.4 0.0 reduce-scatter.2.cloned.1.call-start
  29.5 0.1 compare_reduce_fusion.2
  29.7 0.6 gather_fusion
  30.3 0.1 broadcast_select_fusion
  30.3 172.7 %all-to-all-done = f32[32,8,3840]{2,1,0:T(8,128)} async-done(((f32[32,8,3840]{2,1,0:T(8,128)}), f32[32,8,3840]{2,1,0:T(8,128)}, u32[]{:S(2)}, u32[]{:S(2)}) %all-to-all-start) | async-done | bytes 3932192 | tf_op jit(solution)/shard_map/all_to_all | solution.py:37
  203.1 6.1 %reshape_reshape.3 = f32[256,5,768]{2,1,0:T(8,128)} reshape(f32[32,8,3840]{2,1,0:T(8,128)} %all-to-all-done) | data formatting | bytes 7864320 | tf_op jit(solution)/shard_map/reshape;reshape | solution.py:39
  209.2 9.6 %fusion.2 = f32[5,256,384]{2,1,0:T(8,128)S(1)} fusion(f32[256,5,768]{2,1,0:T(8,128)} %reshape_reshape.3, f32[384,768]{1,0:T(8,128)S(1)} %copy-done), kind=kOutput, calls=%fused_computation.5 | convolution fusion | flops 4529848320 | bytes 7077888 | tf_op jit(solution)/shard_map/kmj,ij->mki/dot_general | solution.py:40
  218.8 1.3 copy-done.1
  220.1 0.1 slice.20
  220.1 0.6 gather_fusion.1
  220.8 2.5 fusion.6
  223.3 1.4 pad_maximum_fusion
  224.7 0.0 reduce-scatter.2.cloned.1.call-update
  224.7 0.7 copy-done.3
  225.4 0.1 compare_reduce_fusion.3
  225.5 90.2 %reduce-scatter.2.cloned.1.call-done = f32[5,16,384]{2,1,0:T(8,128)} async-done(((f32[5,256,384]{2,1,0:T(8,128)}), f32[5,16,384]{2,1,0:T(8,128)}) %reduce-scatter.2.cloned.1.call-update) | async-done | bytes 122896 | tf_op jit(solution)/shard_map/reduce_scatter | solution.py:50
  315.7 1.5 slice_multiply_fusion
  317.2 1.4 slice_multiply_fusion.1
  (19 shorter events, 0.1 us)
Async XLA Ops:
  7.2 202.0 %copy-start = (f32[384,768]{1,0:T(8,128)S(1)}, f32[384,768]{1,0:T(8,128)}, u32[]{:S(2)}) copy-start(f32[384,768]{1,0:T(8,128)} %param.7) | copy-start | bytes 3538948
  12.8 16.7 %copy-start.2 = (s32[3,36]{1,0:T(4,128)S(1)}, s32[3,36]{1,0:T(4,128)}, u32[]{:S(2)}) copy-start(s32[3,36]{1,0:T(4,128)} %param.10) | copy-start | bytes 1300
  12.8 16.9 %copy-start.4 = (s32[2]{0:T(128)S(1)}, s32[2]{0:T(128)}, u32[]{:S(2)}) copy-start(s32[2]{0:T(128)} %param.12) | copy-start | bytes 28
  12.8 190.3 %all-to-all-start = ((f32[32,8,3840]{2,1,0:T(8,128)}), f32[32,8,3840]{2,1,0:T(8,128)}, u32[]{:S(2)}, u32[]{:S(2)}) async-start(f32[32,8,3840]{2,1,0:T(8,128)} %stack.3), calls=%async_computation | async-start | bytes 7864320 | tf_op jit(solution)/shard_map/all_to_all | solution.py:37
  29.4 286.3 %reduce-scatter.2.cloned.1.call-start = ((), (), s32[]{:S(2)}) async-start(), calls=%async_computation.2 | async-start | bytes 2088960 | tf_op jit(solution)/shard_map/reduce_scatter | solution.py:50
  218.8 1.3 copy-start.1
  224.7 0.7 copy-start.3
Sparse Core Ops, SparseCore 0:
  224.8 90.8 reduce-scatter.1
